TPU v7x, 256 devices: a whole 4x4x8 slice. The times are simulated.
256 devices in a mesh: dp: 8 (over y, z_lo), seq: 32 (over z_hi, x, core).
Axes of the slice: x: 4, y: 4, z: 8 (z_hi: 4, z_lo: 2; z = z_hi * 2 + z_lo), core: 2. Of those that a mesh axis runs over, the one named last changes fastest.
Arguments:
- tokens: bfloat16 [8, 256, 128, 512], P('dp', None, 'seq'), may hold values from -6 to 6
- patch_mask: int32 [8, 256, 128], P('dp', None, 'seq'), may hold values 0 or 1
- mask_token: float32 [512], replicated, may hold values from -6 to 6
- gain: float32 [512], replicated, may hold values from 0.1 to 1.9
- w_qkv: bfloat16 [512, 1536], replicated, may hold values from -0.25 to 0.25
- w_out: bfloat16 [512, 512], replicated, may hold values from -0.25 to 0.25
- block_ids: int32 [256], replicated, may hold values from 0 to 3, as said below
- temporal_mask: int32 [8, 8], replicated, may hold values from 0 to 1, as said below
- cotangent: bfloat16 [8, 256, 128, 512], P('dp', None, 'seq'), may hold values from -6 to 6
Outputs:
- layer_out: bfloat16 [8, 256, 128, 512], P('dp', None, 'seq')
- qkv_grad: float32 [1536, 512], P('seq')
- out_grad: float32 [512, 512], P('seq')
Inputs may be any that keep to these rules, and one draw needn't show every extreme that they name: `block_ids`: each block id is held by exactly 64 electrodes. `temporal_mask`: every diagonal entry is 1.
All inputs are finite; a program needn't handle non-finite values. No bound on the sum of `patch_mask` on one device may be relied on, other than what follows from the above.
Results may differ from a plain program's by a relative error of at most 0.0092.
Values may be sent and summed in bfloat16 or wider, within the bound.
No kernel may reach another device: no remote copies, remote signals or barrier semaphores. Data moves between devices by JAX's collectives and lax.ppermute only.
A program may use at most 128 MiB of HBM per device.

v0:
```python
import math

import jax
import jax.numpy as jnp
from jax import lax
from jax.sharding import PartitionSpec as P

P_SIZE = 128
HEADS = 8
HEAD_DIM = 64
EB = 64
TB = 16


NORM_EPS = 1e-05


def normed_input(tokens, patch_mask, mask_token, gain):
    masked = jnp.where(patch_mask[..., None] == 1, mask_token, tokens.astype(jnp.float32))
    row_mean = jnp.mean(masked, axis=-1, keepdims=True)
    centred = masked - row_mean
    spread = jnp.mean(centred * centred, axis=-1, keepdims=True)
    normed = (centred * lax.rsqrt(spread + NORM_EPS) * gain).astype(jnp.bfloat16)
    return (masked, normed)


def forward_attend(queries, key_rows, values, allowed, factor):
    scores = (
        jnp.einsum("anhd,amhd->ahnm", queries, key_rows, preferred_element_type=jnp.float32)
        * factor
    )
    exponent = jnp.exp(scores) * allowed
    weights = exponent / jnp.sum(exponent, axis=-1, keepdims=True)
    rounded = weights.astype(jnp.bfloat16)
    output = jnp.einsum(
        "ahnm,amhd->anhd", rounded, values, preferred_element_type=jnp.float32
    ).astype(jnp.bfloat16)
    return (output, weights, rounded)


def backward_attend(queries, key_rows, values, weights, rounded, grad_out, factor):
    grad_values = jnp.einsum(
        "ahnm,anhd->amhd", rounded, grad_out, preferred_element_type=jnp.float32
    ).astype(jnp.bfloat16)
    grad_weights = jnp.einsum(
        "anhd,amhd->ahnm", grad_out, values, preferred_element_type=jnp.float32
    )
    inner_sum = jnp.sum(grad_weights * weights, axis=-1, keepdims=True)
    grad_scores = (weights * (grad_weights - inner_sum)).astype(jnp.bfloat16)
    grad_queries = (
        jnp.einsum("ahnm,amhd->anhd", grad_scores, key_rows, preferred_element_type=jnp.float32)
        * factor
    ).astype(jnp.bfloat16)
    grad_keys = (
        jnp.einsum("ahnm,anhd->amhd", grad_scores, queries, preferred_element_type=jnp.float32)
        * factor
    ).astype(jnp.bfloat16)
    return (grad_queries, grad_keys, grad_values)


def to_blocks(tensor, block_order, block_size):
    record_count, electrodes, local_patches = tensor.shape[:3]
    trailing = tensor.shape[3:]
    picked = jnp.take(tensor, block_order, axis=1)
    picked = picked.reshape(
        (record_count, electrodes // block_size, block_size, local_patches) + trailing
    )
    picked = jnp.moveaxis(picked, 3, 2)
    return picked.reshape(
        (record_count * (electrodes // block_size) * local_patches, block_size) + trailing
    )


def from_blocks(tensor, inverse, record_count, electrodes, local_patches):
    block_size = tensor.shape[1]
    trailing = tensor.shape[2:]
    restored = tensor.reshape(
        (record_count, electrodes // block_size, local_patches, block_size) + trailing
    )
    restored = jnp.moveaxis(restored, 2, 3).reshape(
        (record_count, electrodes, local_patches) + trailing
    )
    return jnp.take(restored, inverse, axis=1)


def shards(tokens, patch_mask, mask_token, gain, w_qkv, w_out, block_ids, temporal_mask, cotangent):
    record_count, electrodes, local_patches, model_width = tokens.shape
    half_width = model_width // 2
    heads_half = HEADS // 2
    factor = HEAD_DIM ** (-0.5)
    block_order = jnp.argsort(block_ids, stable=True)
    inverse = jnp.argsort(block_order, stable=True)
    onehot = (jnp.arange(P_SIZE)[:, None] // TB == jnp.arange(P_SIZE // TB)[None, :]).astype(
        jnp.float32
    )
    time_allowed = jnp.dot(jnp.dot(onehot, temporal_mask.astype(jnp.float32)), onehot.T)
    same_block = jnp.ones((EB, EB), jnp.float32)
    masked, normed = normed_input(tokens, patch_mask, mask_token, gain)
    normed_flat = normed.reshape(-1, model_width)
    local_columns = 3 * model_width
    projected = jnp.dot(normed_flat, w_qkv, preferred_element_type=jnp.float32).astype(jnp.bfloat16)
    projected = projected.reshape(
        record_count, electrodes, local_patches, local_columns // half_width, heads_half, HEAD_DIM
    )
    spatial = to_blocks(projected[:, :, :, :3], block_order, EB)
    space_out, space_weights, space_rounded = forward_attend(
        spatial[:, :, 0], spatial[:, :, 1], spatial[:, :, 2], same_block, factor
    )
    time_part = projected[:, :, :, 3:].reshape(
        record_count, electrodes, local_patches, 3 * half_width
    )
    regrouped = lax.all_to_all(time_part, "seq", split_axis=1, concat_axis=2, tiled=True)
    items = regrouped.shape[0]
    owned = regrouped.shape[1]
    split_heads = regrouped.reshape(items * owned, P_SIZE, 3, heads_half, HEAD_DIM)
    time_out, time_weights, time_rounded = forward_attend(
        split_heads[:, :, 0], split_heads[:, :, 1], split_heads[:, :, 2], time_allowed, factor
    )
    time_out = time_out.reshape(items, owned, P_SIZE, half_width)
    time_back = lax.all_to_all(time_out, "seq", split_axis=2, concat_axis=1, tiled=True)
    space_back = from_blocks(space_out, inverse, record_count, electrodes, local_patches).reshape(
        record_count, electrodes, local_patches, half_width
    )
    attended = jnp.concatenate([space_back, time_back], axis=-1)
    attended_flat = attended.reshape(-1, model_width)
    layer_out = (
        masked.reshape(-1, model_width)
        + jnp.dot(attended_flat, w_out, preferred_element_type=jnp.float32)
    ).astype(jnp.bfloat16)
    layer_out = layer_out.reshape(tokens.shape)
    cot_flat = cotangent.reshape(-1, model_width)
    out_grad = jnp.einsum("tc,td->cd", cot_flat, attended_flat, preferred_element_type=jnp.float32)
    attended_grad = jnp.einsum(
        "td,cd->tc", cot_flat, w_out, preferred_element_type=jnp.float32
    ).astype(jnp.bfloat16)
    attended_grad = attended_grad.reshape(record_count, electrodes, local_patches, model_width)
    space_grad = to_blocks(
        attended_grad[..., :half_width].reshape(
            record_count, electrodes, local_patches, heads_half, HEAD_DIM
        ),
        block_order,
        EB,
    )
    space_grads = backward_attend(
        spatial[:, :, 0],
        spatial[:, :, 1],
        spatial[:, :, 2],
        space_weights,
        space_rounded,
        space_grad,
        factor,
    )
    spatial_grad = from_blocks(
        jnp.stack(space_grads, axis=2), inverse, record_count, electrodes, local_patches
    )
    spatial_grad = spatial_grad.reshape(-1, 3 * half_width)
    time_grad = lax.all_to_all(
        attended_grad[..., half_width:], "seq", split_axis=1, concat_axis=2, tiled=True
    )
    owned = time_grad.shape[1]
    split_heads = regrouped.reshape(record_count * owned, P_SIZE, 3, heads_half, HEAD_DIM)
    unused_out, time_weights, time_rounded = forward_attend(
        split_heads[:, :, 0], split_heads[:, :, 1], split_heads[:, :, 2], time_allowed, factor
    )
    time_grads = backward_attend(
        split_heads[:, :, 0],
        split_heads[:, :, 1],
        split_heads[:, :, 2],
        time_weights,
        time_rounded,
        time_grad.reshape(record_count * owned, P_SIZE, heads_half, HEAD_DIM),
        factor,
    )
    temporal_grad = jnp.stack(time_grads, axis=2).reshape(
        record_count, owned, P_SIZE, 3 * half_width
    )
    temporal_back = lax.all_to_all(
        temporal_grad, "seq", split_axis=2, concat_axis=1, tiled=True
    ).reshape(-1, 3 * half_width)
    projected_grad = jnp.concatenate([spatial_grad, temporal_back], axis=1)
    qkv_grad = jnp.einsum(
        "tc,td->cd", projected_grad, normed_flat, preferred_element_type=jnp.float32
    )
    groups = lax.axis_size("seq")
    grad_scale = 1.0 / math.sqrt(
        record_count * lax.axis_size("dp") * electrodes * local_patches * groups
    )
    rows_qkv = qkv_grad.shape[0] // groups
    rows_out = model_width // groups
    total_qkv, total_out = lax.psum((qkv_grad, out_grad), ("dp", "seq"))
    position = lax.axis_index("seq")
    share_qkv = lax.dynamic_slice_in_dim(total_qkv, position * rows_qkv, rows_qkv, 0)
    share_out = lax.dynamic_slice_in_dim(total_out, position * rows_out, rows_out, 0)
    return (layer_out, share_qkv * grad_scale, share_out * grad_scale)


def solution(mesh):
    return jax.shard_map(
        shards,
        mesh=mesh,
        in_specs=(
            P("dp", None, "seq", None),
            P("dp", None, "seq"),
            P(),
            P(),
            P(),
            P(),
            P(),
            P(),
            P("dp", None, "seq", None),
        ),
        out_specs=(P("dp", None, "seq", None), P("seq", None), P("seq", None)),
        check_vma=False,
    )
```

profile of v0, /device:TPU:2, one launch (start us, length us, event | category | flops | bytes accessed | tf_op | source)
XLA Modules:
  0.0 517.9 jit_solution(974324439609821038)
XLA Ops:
  14.7 11.7 %all-to-all-start.2 = ((bf16[1,256,4,256]{3,2,0,1:T(4,128)(2,1)}), bf16[1,256,4,256]{3,2,0,1:T(4,128)(2,1)S(1)}, u32[]{:S(2)}, u32[]{:S(2)}) async-start(bf16[1,256,4,256]{3,2,0,1:T(4,128)(2,1)} %slice.65), calls=%async_computation.2 | async-start | bytes 1048576 | tf_op jit(solution)/shard_map/all_to_all | solution.py:157
  29.4 2.9 multiply_convert_fusion.4
  33.7 3.4 convolution_convert_fusion
  37.2 10.5 %reshape.200 = bf16[1,256,4,6,4,64]{5,4,3,2,1,0:T(4,128)(2,1)} reshape(bf16[1024,1536]{1,0:T(8,128)(2,1)} %convolution_convert_fusion) | data formatting | bytes 6291456 | tf_op jit(solution)/shard_map/reshape | solution.py:102
  47.7 7.4 %slice_bitcast_fusion = (bf16[256,4,3,4,64]{4,3,2,1,0:T(4,128)(2,1)}, bf16[1,256,4,3,4,64]{5,4,3,2,1,0:T(4,128)(2,1)}) fusion(bf16[1,256,4,6,4,64]{5,4,3,2,1,0:T(4,128)(2,1)} %reshape.200), kind=kLoop, calls=%fused_computation.5 | loop fusion | bytes 6291456 | tf_op jit(solution)/shard_map/jit(_take)/Arg_0.11 | solution.py:64
  55.1 4.5 copy.128
  61.9 10.2 %all-to-all-start = ((bf16[1,256,4,768]{3,2,0,1:T(4,128)(2,1)}), bf16[1,256,4,768]{3,2,0,1:T(4,128)(2,1)S(1)}, u32[]{:S(2)}, u32[]{:S(2)}) async-start(bf16[1,256,4,768]{3,2,0,1:T(4,128)(2,1)} %copy.129), calls=%async_computation | async-start | bytes 3145728 | tf_op jit(solution)/shard_map/all_to_all | solution.py:112
  73.1 3.2 sort.31
  76.3 6.8 %gather_fusion = bf16[256,4,3,4,64]{4,3,2,1,0:T(4,128)(2,1)} fusion(bf16[256,4,3,4,64]{4,3,2,1,0:T(4,128)(2,1)} %get-tuple-element.23, s32[1024]{0:T(1024)S(1)} %pad_clamp_fusion.1), kind=kCustom, calls=%fused_computation.clone | custom fusion | bytes 3146752 | tf_op jit(solution)/shard_map/jit(_take)/gather | solution.py:64
  83.1 3.8 bitcast_select_fusion.1
  86.9 2.6 copy.123
  107.7 4.1 all-to-all-done
  112.2 3.3 reshape.206
  115.5 4.3 fusion.48
  127.5 5.8 %all-to-all-start.1 = ((bf16[1,8,128,256]{3,1,0,2:T(8,128)(2,1)}), bf16[1,8,128,256]{3,1,0,2:T(8,128)(2,1)}, u32[]{:S(2)}, u32[]{:S(2)}) async-start(bf16[1,8,128,256]{3,1,0,2:T(8,128)(2,1)} %copy.137), calls=%async_computation.1 | async-start | bytes 1048576 | tf_op jit(solution)/shard_map/all_to_all | solution.py:120
  140.8 9.4 %all-to-all-done.1 = bf16[1,8,128,256]{3,1,0,2:T(8,128)(2,1)} async-done(((bf16[1,8,128,256]{3,1,0,2:T(8,128)(2,1)}), bf16[1,8,128,256]{3,1,0,2:T(8,128)(2,1)}, u32[]{:S(2)}, u32[]{:S(2)}) %all-to-all-start.1) | async-done | bytes 524320 | tf_op jit(solution)/shard_map/all_to_all | solution.py:120
  150.2 5.5 %all-to-all-start.3 = ((bf16[1,8,128,768]{3,1,0,2:T(8,128)(2,1)}), bf16[1,8,128,768]{3,1,0,2:T(8,128)(2,1)S(1)}, u32[]{:S(2)}, u32[]{:S(2)}) async-start(bf16[1,8,128,768]{3,1,0,2:T(8,128)(2,1)} %copy.164), calls=%async_computation.3 | async-start | bytes 3145728 | tf_op jit(solution)/shard_map/all_to_all | solution.py:177
  155.8 3.4 convolution_convert_fusion.1
  162.6 3.2 sort.32
  165.7 3.3 copy.153
  176.3 2.7 multiply_convert_fusion.2
  181.5 5.7 %maximum_bitcast_fusion = bf16[1,4,64,4,3,4,64]{2,1,6,5,4,3,0:T(4,128)(2,1)} fusion(bf16[1,4,4,64,1,4,64]{3,1,6,5,4,2,0:T(4,128)(2,1)S(1)} %copy-done.9, bf16[1,4,4,64,1,4,64]{3,1,6,5,4,2,0:T(4,128)(2,1)} %copy.152, bf16[1,4,4,64,1,4,64]{3,1,6,5,4,2,0:T(4,128)(2,1)} %copy.151), kind=kLoop, calls=%fused_computation.6 | loop fusion | flops 1572864 | bytes 3145728 | tf_op jit(solution)/shard_map/transpose | solution.py:80
  187.2 9.4 %copy.190 = bf16[1,4,64,4,3,4,64]{6,5,4,3,2,1,0:T(4,128)(2,1)} copy(bf16[1,4,64,4,3,4,64]{2,1,6,5,4,3,0:T(4,128)(2,1)} %maximum_bitcast_fusion) | data formatting | bytes 3145728 | tf_op jit(solution)/shard_map/reshape | solution.py:80
  199.0 6.7 %gather_fusion.3 = bf16[256,4,3,4,64]{4,3,2,1,0:T(4,128)(2,1)} fusion(bf16[256,4,3,4,64]{4,3,2,1,0:T(4,128)(2,1)} %bitcast.159, s32[1024]{0:T(1024)S(1)} %pad_clamp_fusion), kind=kCustom, calls=%fused_computation.2.clone | custom fusion | bytes 3146752 | tf_op jit(solution)/shard_map/jit(_take)/gather | solution.py:83
  205.7 5.2 %bitcast_select_fusion = bf16[1,256,4,3,4,64]{5,4,3,2,1,0:T(4,128)(2,1)} fusion(bf16[256,4,3,4,64]{4,3,2,1,0:T(4,128)(2,1)} %gather_fusion.3, pred[256]{0:T(512)(128)(4,1)S(1)} %compare_and_fusion), kind=kLoop, calls=%fused_computation.11 | loop fusion | flops 786432 | bytes 3145984 | tf_op jit(solution)/shard_map/jit(_take)/select_n | solution.py:83
  210.9 5.7 %reshape.215 = bf16[1024,768]{1,0:T(8,128)(2,1)} reshape(bf16[1,256,4,3,4,64]{5,4,3,2,1,0:T(4,128)(2,1)} %bitcast_select_fusion) | data formatting | bytes 3145728 | tf_op jit(solution)/shard_map/reshape | solution.py:156
  222.4 3.3 convolution_bitcast_fusion
  227.6 2.7 reshape.218
  230.4 5.2 %fusion = f32[1536,512]{1,0:T(8,128)} fusion(bf16[1024,512]{1,0:T(8,128)(2,1)} %copy-done.14, bf16[1024,768]{1,0:T(8,128)(2,1)S(1)} %reshape.218, bf16[1024,768]{1,0:T(8,128)(2,1)} %reshape.215), kind=kOutput, calls=%fused_computation.7 | convolution fusion | flops 1616904192 | bytes 7340032 | tf_op jit(solution)/shard_map/tc,td->cd/dot_general | solution.py:181
  236.3 2.9 reshape.198
  241.5 2.7 add_convert_fusion
  245.3 262.2 %all-reduce.3.cloned.1.call-done = (f32[1536,512]{1,0:T(8,128)}, f32[512,512]{0,1:T(8,128)}) async-done(((f32[1536,512]{1,0:T(8,128)}, f32[512,512]{0,1:T(8,128)}), (f32[1536,512]{1,0:T(8,128)}, f32[512,512]{0,1:T(8,128)})) %all-reduce.3.cloned.1.call-update) | async-done | bytes 4194320 | tf_op jit(solution)/shard_map/psum | solution.py:190
  (125 shorter events, 79.3 us)
Async XLA Ops:
  7.2 26.5 %copy-start = (bf16[512,1536]{1,0:T(8,128)(2,1)S(1)}, bf16[512,1536]{1,0:T(8,128)(2,1)}, u32[]{:S(2)}) copy-start(bf16[512,1536]{1,0:T(8,128)(2,1)} %param.17) | copy-start | bytes 4718596
  7.2 1.5 copy-start.18
  10.4 16.0 %copy-start.21 = (s32[1,256,4]{1,2,0:T(4,128)S(1)}, s32[1,256,4]{1,2,0:T(4,128)}, u32[]{:S(2)}) copy-start(s32[1,256,4]{1,2,0:T(4,128)} %param.14) | copy-start | bytes 12292
  10.4 16.2 %copy-start.3 = (bf16[1,256,4,512]{3,2,1,0:T(4,128)(2,1)S(1)}, bf16[1,256,4,512]{3,2,1,0:T(4,128)(2,1)}, u32[]{:S(2)}) copy-start(bf16[1,256,4,512]{3,2,1,0:T(4,128)(2,1)} %param.13) | copy-start | bytes 3145732
  10.4 16.2 %copy-start.20 = (f32[512]{0:T(512)S(1)}, f32[512]{0:T(512)}, u32[]{:S(2)}) copy-start(f32[512]{0:T(512)} %param.15) | copy-start | bytes 6148
  14.7 14.7 %copy-start.22 = (f32[512]{0:T(512)S(1)}, f32[512]{0:T(512)}, u32[]{:S(2)}) copy-start(f32[512]{0:T(512)} %param.16) | copy-start | bytes 6148
  14.7 47.2 %all-to-all-start.2 = ((bf16[1,256,4,256]{3,2,0,1:T(4,128)(2,1)}), bf16[1,256,4,256]{3,2,0,1:T(4,128)(2,1)S(1)}, u32[]{:S(2)}, u32[]{:S(2)}) async-start(bf16[1,256,4,256]{3,2,0,1:T(4,128)(2,1)} %slice.65), calls=%async_computation.2 | async-start | bytes 1048576 | tf_op jit(solution)/shard_map/all_to_all | solution.py:157
  33.7 3.4 copy-start.14
  61.9 10.2 %copy-start.7 = (bf16[1,256,4,512]{3,2,1,0:T(4,128)(2,1)S(1)}, bf16[1,256,4,512]{3,2,1,0:T(4,128)(2,1)}, u32[]{:S(2)}) copy-start(bf16[1,256,4,512]{3,2,1,0:T(4,128)(2,1)} %reshape.210) | copy-start | bytes 3145732
  61.9 11.2 %copy-start.23 = (s32[256]{0:T(256)S(1)}, s32[256]{0:T(256)}, u32[]{:S(2)}) copy-start(s32[256]{0:T(256)} %param.19) | copy-start | bytes 3076
  61.9 11.2 %copy-start.10 = (bf16[1,256,4,256]{3,2,0,1:T(4,128)(2,1)}, bf16[1,256,4,256]{3,2,0,1:T(4,128)(2,1)S(1)}, u32[]{:S(2)}) copy-start(bf16[1,256,4,256]{3,2,0,1:T(4,128)(2,1)S(1)} %all-to-all-done.2) | copy-start | bytes 1572868
  61.9 49.9 %all-to-all-start = ((bf16[1,256,4,768]{3,2,0,1:T(4,128)(2,1)}), bf16[1,256,4,768]{3,2,0,1:T(4,128)(2,1)S(1)}, u32[]{:S(2)}, u32[]{:S(2)}) async-start(bf16[1,256,4,768]{3,2,0,1:T(4,128)(2,1)} %copy.129), calls=%async_computation | async-start | bytes 3145728 | tf_op jit(solution)/shard_map/all_to_all | solution.py:112
  86.9 2.6 copy-start.12
  95.4 4.1 copy-start.24
  99.5 4.6 copy-start.15
  99.8 2.5 copy-start.2
  102.3 1.8 copy-start.4
  104.1 2.1 copy-start.11
  123.3 1.7 copy-start.19
  125.0 1.3 copy-start.5
  127.5 22.7 %all-to-all-start.1 = ((bf16[1,8,128,256]{3,1,0,2:T(8,128)(2,1)}), bf16[1,8,128,256]{3,1,0,2:T(8,128)(2,1)}, u32[]{:S(2)}, u32[]{:S(2)}) async-start(bf16[1,8,128,256]{3,1,0,2:T(8,128)(2,1)} %copy.137), calls=%async_computation.1 | async-start | bytes 1048576 | tf_op jit(solution)/shard_map/all_to_all | solution.py:120
  133.2 2.6 copy-start.6
  140.8 15.0 %copy-start.16 = (bf16[1,4,4,64,4,64]{5,3,4,2,1,0:T(8,128)(2,1)S(1)}, bf16[1,4,4,64,4,64]{5,3,4,2,1,0:T(8,128)(2,1)}, u32[]{:S(2)}) copy-start(bf16[1,4,4,64,4,64]{5,3,4,2,1,0:T(8,128)(2,1)} %copy-done.15) | copy-start | bytes 1572868
  150.2 75.5 %all-to-all-start.3 = ((bf16[1,8,128,768]{3,1,0,2:T(8,128)(2,1)}), bf16[1,8,128,768]{3,1,0,2:T(8,128)(2,1)S(1)}, u32[]{:S(2)}, u32[]{:S(2)}) async-start(bf16[1,8,128,768]{3,1,0,2:T(8,128)(2,1)} %copy.164), calls=%async_computation.3 | async-start | bytes 3145728 | tf_op jit(solution)/shard_map/all_to_all | solution.py:177
  155.7 351.8 %all-reduce.3.cloned.1.call-start = ((), (), s32[]{:S(2)}) async-start(), calls=%async_computation.4 | async-start | bytes 8388608 | tf_op jit(solution)/shard_map/psum | solution.py:190
  155.8 3.4 copy-start.17
  165.7 3.3 copy-start.13
  179.0 2.5 copy-start.9
  187.2 9.4 %copy-start.8 = (bf16[1,4,64,4,4,64]{5,4,3,2,1,0:T(4,128)(2,1)S(1)}, bf16[1,4,64,4,4,64]{5,4,3,2,1,0:T(4,128)(2,1)}, u32[]{:S(2)}) copy-start(bf16[1,4,64,4,4,64]{5,4,3,2,1,0:T(4,128)(2,1)} %copy.186) | copy-start | bytes 1572868
  241.5 269.4 %copy-start.1 = (bf16[512,1536]{1,0:T(8,128)(2,1)S(1)}, bf16[512,1536]{1,0:T(8,128)(2,1)}, u32[]{:S(2)}) copy-start(bf16[512,1536]{1,0:T(8,128)(2,1)} %param.17) | copy-start | bytes 4718596
Sparse Core Ops, SparseCore 0:
  235.8 271.6 all-reduce.2
where the time goes:
time: 526 us; the launch traced here: 518 us
  waiting for transfers between devices  276 us (52%)
  local copies, waits for them, and re-layouts  120 us (23%)
  matrix products  37.6 us (7%)
  other arithmetic  36.5 us (7%)
  starting transfers between devices  33.3 us (6%)
  between operations  14.8 us (3%)
    psum x1, waiting for transfers between devices, shards(): total_qkv, total_out = lax.psum((qkv_grad, out_grad), ('dp', 'seq'))  262 us
    reshape x2, local copies, waits for them, and re-layouts, from_blocks(): jnp.moveaxis(restored, 2, 3)  11.9 us
    all_to_all x1, starting transfers between devices, shards(): lax.all_to_all(attended_grad[..., half_width:], 'seq', split_axis=1, conc...  11.7 us
  transfers between devices with their start and end apart: 5, of which 3 were waited for; matrix products, arithmetic and copies ran while one was open for 30% of the time, Pallas kernels for 0%

commit v1 on v0

--- a/solution.py
+++ b/solution.py
@@ -187,11 +187,16 @@
     )
     rows_qkv = qkv_grad.shape[0] // groups
     rows_out = model_width // groups
-    total_qkv, total_out = lax.psum((qkv_grad, out_grad), ("dp", "seq"))
-    position = lax.axis_index("seq")
-    share_qkv = lax.dynamic_slice_in_dim(total_qkv, position * rows_qkv, rows_qkv, 0)
-    share_out = lax.dynamic_slice_in_dim(total_out, position * rows_out, rows_out, 0)
-    return (layer_out, share_qkv * grad_scale, share_out * grad_scale)
+    stacked = jnp.concatenate(
+        [
+            qkv_grad.reshape(groups, rows_qkv, model_width),
+            out_grad.reshape(groups, rows_out, model_width),
+        ],
+        axis=1,
+    )
+    share = lax.psum_scatter(stacked, "seq", scatter_dimension=0, tiled=True)
+    share = lax.psum(share, "dp").reshape(rows_qkv + rows_out, model_width)
+    return (layer_out, share[:rows_qkv] * grad_scale, share[rows_qkv:] * grad_scale)
 
 
 def solution(mesh):

time: 526 us -> 445 us (0.85)
  waiting for transfers between devices: 276 us -> 179 us
  local copies, waits for them, and re-layouts: 120 us -> 134 us
  matrix products: 37.6 us -> 29.3 us
  other arithmetic: 36.5 us -> 42 us
    psum x1, waiting for transfers between devices: 262 us -> 75.9 us  [shards(): share = lax.psum(share, 'dp').reshape(rows_qkv + rows_out, model_width)]
    reduce_scatter x0 -> x1, waiting for transfers between devices: none -> 94 us  [shards(): share = lax.psum_scatter(stacked, 'seq', scatter_dimension=0, tiled=True)]
  transfers between devices with their start and end apart: 5 -> 6, of which waited for: 3 -> 3; matrix products, arithmetic and copies ran while one was open for 30% -> 36% of each run, Pallas kernels for 0% -> 0%
where the time goes in v1:
time: 445 us; the launch traced here: 436 us
  waiting for transfers between devices  179 us (40%)
  local copies, waits for them, and re-layouts  134 us (30%)
  other arithmetic  42 us (9%)
  starting transfers between devices  37.3 us (8%)
  matrix products  29.3 us (7%)
  between operations  14.8 us (3%)
    reduce_scatter x1, waiting for transfers between devices, shards(): share = lax.psum_scatter(stacked, 'seq', scatter_dimension=0, tiled=True)  94 us
    psum x1, waiting for transfers between devices, shards(): share = lax.psum(share, 'dp').reshape(rows_qkv + rows_out, model_width)  75.9 us
    all_to_all x1, starting transfers between devices, shards(): lax.all_to_all(attended_grad[..., half_width:], 'seq', split_axis=1, conc...  11.7 us
    reshape x2, local copies, waits for them, and re-layouts, from_blocks(): jnp.moveaxis(restored, 2, 3)  11.4 us
    reshape x1, local copies, waits for them, and re-layouts, shards(): projected.reshape(record_count, electrodes, local_patches, local_columns...  10.5 us
    gather x2, local copies, waits for them, and re-layouts, to_blocks(): picked = jnp.take(tensor, block_order, axis=1)  10.4 us
    gather x2, local copies, waits for them, and re-layouts, from_blocks(): return jnp.take(restored, inverse, axis=1)  10.4 us
    all_to_all x1, starting transfers between devices, shards(): lax.all_to_all(time_part, 'seq', split_axis=1, concat_axis=2, tiled=True)  10.1 us
  transfers between devices with their start and end apart: 6, of which 3 were waited for; matrix products, arithmetic and copies ran while one was open for 36% of the time, Pallas kernels for 0%

profile of v1, /device:TPU:2, one launch (start us, length us, event | category | flops | bytes accessed | tf_op | source)
XLA Modules:
  0.0 436.5 jit_solution(2369056662675700216)
XLA Ops:
  14.7 11.7 %all-to-all-start.2 = ((bf16[1,256,4,256]{3,2,0,1:T(4,128)(2,1)}), bf16[1,256,4,256]{3,2,0,1:T(4,128)(2,1)S(1)}, u32[]{:S(2)}, u32[]{:S(2)}) async-start(bf16[1,256,4,256]{3,2,0,1:T(4,128)(2,1)} %slice.75), calls=%async_computation.2 | async-start | bytes 1048576 | tf_op jit(solution)/shard_map/all_to_all | solution.py:157
  29.4 2.9 multiply_convert_fusion.4
  33.7 3.5 convolution_convert_fusion
  37.2 10.5 %reshape.212 = bf16[1,256,4,6,4,64]{5,4,3,2,1,0:T(4,128)(2,1)} reshape(bf16[1024,1536]{1,0:T(8,128)(2,1)} %convolution_convert_fusion) | data formatting | bytes 6291456 | tf_op jit(solution)/shard_map/reshape | solution.py:102
  47.7 7.6 %slice_bitcast_fusion = (bf16[256,4,3,4,64]{4,3,2,1,0:T(4,128)(2,1)}, bf16[1,256,4,3,4,64]{5,4,3,2,1,0:T(4,128)(2,1)}) fusion(bf16[1,256,4,6,4,64]{5,4,3,2,1,0:T(4,128)(2,1)} %reshape.212), kind=kLoop, calls=%fused_computation.6 | loop fusion | bytes 6291456 | tf_op jit(solution)/shard_map/jit(_take)/Arg_0.11 | solution.py:64
  55.2 4.5 %copy.127 = bf16[1,256,4,3,4,64]{1,5,4,3,2,0:T(8,128)(2,1)S(1)} copy(bf16[1,256,4,3,4,64]{5,4,3,2,1,0:T(4,128)(2,1)} %get-tuple-element.10) | data formatting | bytes 3145728 | tf_op jit(solution)/shard_map/slice | solution.py:109
  62.1 3.2 sort.31
  66.1 10.1 %all-to-all-start = ((bf16[1,256,4,768]{3,2,0,1:T(4,128)(2,1)}), bf16[1,256,4,768]{3,2,0,1:T(4,128)(2,1)S(1)}, u32[]{:S(2)}, u32[]{:S(2)}) async-start(bf16[1,256,4,768]{3,2,0,1:T(4,128)(2,1)} %copy.128), calls=%async_computation | async-start | bytes 3145728 | tf_op jit(solution)/shard_map/all_to_all | solution.py:112
  79.3 6.7 %gather_fusion = bf16[256,4,3,4,64]{4,3,2,1,0:T(4,128)(2,1)} fusion(bf16[256,4,3,4,64]{4,3,2,1,0:T(4,128)(2,1)} %get-tuple-element.9, s32[1024]{0:T(1024)S(1)} %pad_clamp_fusion.1), kind=kCustom, calls=%fused_computation.clone | custom fusion | bytes 3146752 | tf_op jit(solution)/shard_map/jit(_take)/gather | solution.py:64
  86.0 3.8 bitcast_select_fusion.1
  96.0 3.2 sort.32
  99.2 3.7 gather_fusion.1
  109.8 3.7 gather_fusion.2
  113.5 2.8 bitcast_select_fusion.2
  116.3 3.9 copy.186
  120.2 2.8 copy.141
  127.9 3.1 reshape.218
  131.0 4.5 %fusion.46 = (bf16[8,128,1,4,64]{4,3,2,0,1:T(4,128)(2,1)S(1)}, bf16[8,128,1,4,64]{4,3,2,0,1:T(4,128)(2,1)}, bf16[8,128,1,4,64]{4,3,2,0,1:T(4,128)(2,1)}) fusion(bf16[8,128,3,4,64]{4,3,2,0,1:T(4,128)(2,1)} %reshape.218), kind=kLoop, calls=%fused_computation.96 | loop fusion | bytes 3145728 | tf_op jit(solution)/shard_map/slice | solution.py:117
  145.8 9.8 %all-to-all-start.1 = ((bf16[1,8,128,256]{3,1,0,2:T(8,128)(2,1)}), bf16[1,8,128,256]{3,1,0,2:T(8,128)(2,1)}, u32[]{:S(2)}, u32[]{:S(2)}) async-start(bf16[1,8,128,256]{3,1,0,2:T(8,128)(2,1)} %copy.136), calls=%async_computation.1 | async-start | bytes 1048576 | tf_op jit(solution)/shard_map/all_to_all | solution.py:120
  163.3 9.3 %all-to-all-done.1 = bf16[1,8,128,256]{3,1,0,2:T(8,128)(2,1)} async-done(((bf16[1,8,128,256]{3,1,0,2:T(8,128)(2,1)}), bf16[1,8,128,256]{3,1,0,2:T(8,128)(2,1)}, u32[]{:S(2)}, u32[]{:S(2)}) %all-to-all-start.1) | async-done | bytes 524320 | tf_op jit(solution)/shard_map/all_to_all | solution.py:120
  172.6 5.6 %all-to-all-start.3 = ((bf16[1,8,128,768]{3,1,0,2:T(8,128)(2,1)}), bf16[1,8,128,768]{3,1,0,2:T(8,128)(2,1)}, u32[]{:S(2)}, u32[]{:S(2)}) async-start(bf16[1,8,128,768]{3,1,0,2:T(8,128)(2,1)} %copy.163), calls=%async_computation.3 | async-start | bytes 3145728 | tf_op jit(solution)/shard_map/all_to_all | solution.py:177
  193.2 5.6 %maximum_bitcast_fusion = bf16[1,4,64,4,3,4,64]{2,1,6,5,4,3,0:T(4,128)(2,1)} fusion(bf16[1,4,4,64,1,4,64]{3,1,6,5,4,2,0:T(4,128)(2,1)S(1)} %copy-done.10, bf16[1,4,4,64,1,4,64]{3,1,6,5,4,2,0:T(4,128)(2,1)} %copy.151, bf16[1,4,4,64,1,4,64]{3,1,6,5,4,2,0:T(4,128)(2,1)} %copy.150), kind=kLoop, calls=%fused_computation.7 | loop fusion | flops 1572864 | bytes 3145728 | tf_op jit(solution)/shard_map/transpose | solution.py:80
  198.8 9.3 %copy.189 = bf16[1,4,64,4,3,4,64]{6,5,4,3,2,1,0:T(4,128)(2,1)} copy(bf16[1,4,64,4,3,4,64]{2,1,6,5,4,3,0:T(4,128)(2,1)} %maximum_bitcast_fusion) | data formatting | bytes 3145728 | tf_op jit(solution)/shard_map/reshape | solution.py:80
  208.1 6.7 %gather_fusion.3 = bf16[256,4,3,4,64]{4,3,2,1,0:T(4,128)(2,1)} fusion(bf16[256,4,3,4,64]{4,3,2,1,0:T(4,128)(2,1)} %bitcast.168, s32[1024]{0:T(1024)S(1)} %pad_clamp_fusion), kind=kCustom, calls=%fused_computation.2.clone | custom fusion | bytes 3146752 | tf_op jit(solution)/shard_map/jit(_take)/gather | solution.py:83
  214.7 5.2 %bitcast_select_fusion = bf16[1,256,4,3,4,64]{5,4,3,2,1,0:T(4,128)(2,1)} fusion(bf16[256,4,3,4,64]{4,3,2,1,0:T(4,128)(2,1)} %gather_fusion.3, pred[256]{0:T(512)(128)(4,1)S(1)} %compare_and_fusion), kind=kLoop, calls=%fused_computation.9 | loop fusion | flops 786432 | bytes 3145984 | tf_op jit(solution)/shard_map/jit(_take)/select_n | solution.py:83
  219.9 5.8 %reshape.227 = bf16[1024,768]{1,0:T(8,128)(2,1)} reshape(bf16[1,256,4,3,4,64]{5,4,3,2,1,0:T(4,128)(2,1)} %bitcast_select_fusion) | data formatting | bytes 3145728 | tf_op jit(solution)/shard_map/reshape | solution.py:156
  232.2 3.7 maximum_bitcast_fusion.1
  235.9 4.7 %copy.165 = bf16[1536,1024]{1,0:T(8,128)(2,1)} copy(bf16[1536,1024]{0,1:T(8,128)(2,1)} %maximum_bitcast_fusion.1) | data formatting | bytes 6291456 | tf_op jit(solution)/shard_map/tc,td->cd/dot_general | solution.py:181
  240.6 3.8 fusion.47
  247.6 3.0 reshape.210
  252.8 94.0 %reduce-scatter.2.cloned.1.call-done = f32[1,64,512]{2,1,0:T(8,128)} async-done(((f32[32,64,512]{2,1,0:T(8,128)}), f32[1,64,512]{2,1,0:T(8,128)}) %reduce-scatter.2.cloned.1.call-update) | async-done | bytes 131088 | tf_op jit(solution)/shard_map/reduce_scatter | solution.py:197
  350.6 75.9 %all-reduce.2.cloned.1.call-done = f32[1,64,512]{2,1,0:T(8,128)} async-done(((f32[1,64,512]{2,1,0:T(8,128)}), f32[1,64,512]{2,1,0:T(8,128)}) %all-reduce.2.cloned.1.call-update) | async-done | bytes 131088 | tf_op jit(solution)/shard_map/psum | solution.py:198
  (133 shorter events, 87.2 us)
Async XLA Ops:
  7.2 26.5 %copy-start = (bf16[512,1536]{1,0:T(8,128)(2,1)S(1)}, bf16[512,1536]{1,0:T(8,128)(2,1)}, u32[]{:S(2)}) copy-start(bf16[512,1536]{1,0:T(8,128)(2,1)} %param.17) | copy-start | bytes 4718596
  7.2 1.5 copy-start.17
  10.4 16.0 %copy-start.22 = (s32[1,256,4]{1,2,0:T(4,128)S(1)}, s32[1,256,4]{1,2,0:T(4,128)}, u32[]{:S(2)}) copy-start(s32[1,256,4]{1,2,0:T(4,128)} %param.14) | copy-start | bytes 12292
  10.4 16.2 %copy-start.4 = (bf16[1,256,4,512]{3,2,1,0:T(4,128)(2,1)S(1)}, bf16[1,256,4,512]{3,2,1,0:T(4,128)(2,1)}, u32[]{:S(2)}) copy-start(bf16[1,256,4,512]{3,2,1,0:T(4,128)(2,1)} %param.13) | copy-start | bytes 3145732
  10.4 16.2 %copy-start.21 = (f32[512]{0:T(512)S(1)}, f32[512]{0:T(512)}, u32[]{:S(2)}) copy-start(f32[512]{0:T(512)} %param.15) | copy-start | bytes 6148
  14.7 14.7 %copy-start.23 = (f32[512]{0:T(512)S(1)}, f32[512]{0:T(512)}, u32[]{:S(2)}) copy-start(f32[512]{0:T(512)} %param.16) | copy-start | bytes 6148
  14.7 50.6 %all-to-all-start.2 = ((bf16[1,256,4,256]{3,2,0,1:T(4,128)(2,1)}), bf16[1,256,4,256]{3,2,0,1:T(4,128)(2,1)S(1)}, u32[]{:S(2)}, u32[]{:S(2)}) async-start(bf16[1,256,4,256]{3,2,0,1:T(4,128)(2,1)} %slice.75), calls=%async_computation.2 | async-start | bytes 1048576 | tf_op jit(solution)/shard_map/all_to_all | solution.py:157
  59.7 2.4 copy-start.24
  65.3 12.9 %copy-start.5 = (bf16[1,256,4,512]{3,2,1,0:T(4,128)(2,1)S(1)}, bf16[1,256,4,512]{3,2,1,0:T(4,128)(2,1)}, u32[]{:S(2)}) copy-start(bf16[1,256,4,512]{3,2,1,0:T(4,128)(2,1)} %get-tuple-element.14) | copy-start | bytes 3145732
  65.3 0.8 copy-start.11
  66.1 61.4 %all-to-all-start = ((bf16[1,256,4,768]{3,2,0,1:T(4,128)(2,1)}), bf16[1,256,4,768]{3,2,0,1:T(4,128)(2,1)S(1)}, u32[]{:S(2)}, u32[]{:S(2)}) async-start(bf16[1,256,4,768]{3,2,0,1:T(4,128)(2,1)} %copy.128), calls=%async_computation | async-start | bytes 3145728 | tf_op jit(solution)/shard_map/all_to_all | solution.py:112
  90.6 1.6 copy-start.2
  91.4 1.6 copy-start.6
  116.3 6.7 %copy-start.25 = (s32[8,8]{1,0:T(8,128)S(1)}, s32[8,8]{1,0:T(8,128)}, u32[]{:S(2)}) copy-start(s32[8,8]{1,0:T(8,128)} %param.20) | copy-start | bytes 772
  116.3 7.1 %copy-start.12 = (bf16[1,256,4,256]{3,2,0,1:T(4,128)(2,1)S(1)}, bf16[1,256,4,256]{3,2,0,1:T(4,128)(2,1)}, u32[]{:S(2)}) copy-start(bf16[1,256,4,256]{3,2,0,1:T(4,128)(2,1)} %copy-done.11) | copy-start | bytes 1572868
  141.0 1.0 copy-start.19
  141.7 1.8 copy-start.8
  143.5 12.2 %copy-start.18 = (bf16[8,128,4,64]{1,3,2,0:T(8,128)(2,1)S(1)}, bf16[8,128,4,64]{1,3,2,0:T(8,128)(2,1)}, u32[]{:S(2)}) copy-start(bf16[8,128,4,64]{1,3,2,0:T(8,128)(2,1)} %copy.157) | copy-start | bytes 1572868
  145.8 26.8 %all-to-all-start.1 = ((bf16[1,8,128,256]{3,1,0,2:T(8,128)(2,1)}), bf16[1,8,128,256]{3,1,0,2:T(8,128)(2,1)}, u32[]{:S(2)}, u32[]{:S(2)}) async-start(bf16[1,8,128,256]{3,1,0,2:T(8,128)(2,1)} %copy.136), calls=%async_computation.1 | async-start | bytes 1048576 | tf_op jit(solution)/shard_map/all_to_all | solution.py:120
  155.7 2.6 copy-start.9
  163.3 14.9 %copy-start.15 = (bf16[1,4,4,64,4,64]{5,3,4,2,1,0:T(8,128)(2,1)S(1)}, bf16[1,4,4,64,4,64]{5,3,4,2,1,0:T(8,128)(2,1)}, u32[]{:S(2)}) copy-start(bf16[1,4,4,64,4,64]{5,3,4,2,1,0:T(8,128)(2,1)} %copy.141) | copy-start | bytes 1572868
  172.6 56.0 %all-to-all-start.3 = ((bf16[1,8,128,768]{3,1,0,2:T(8,128)(2,1)}), bf16[1,8,128,768]{3,1,0,2:T(8,128)(2,1)}, u32[]{:S(2)}, u32[]{:S(2)}) async-start(bf16[1,8,128,768]{3,1,0,2:T(8,128)(2,1)} %copy.163), calls=%async_computation.3 | async-start | bytes 3145728 | tf_op jit(solution)/shard_map/all_to_all | solution.py:177
  178.1 168.6 %reduce-scatter.2.cloned.1.call-start = ((), (), s32[]{:S(2)}) async-start(), calls=%async_computation.5 | async-start | bytes 4325376 | tf_op jit(solution)/shard_map/reduce_scatter | solution.py:197
  178.2 4.3 copy-start.3
  180.7 1.9 copy-start.7
  190.7 2.5 copy-start.10
  219.9 6.9 %copy-start.13 = (bf16[1,256,4,512]{3,2,1,0:T(4,128)(2,1)S(1)}, bf16[1,256,4,512]{3,2,1,0:T(4,128)(2,1)}, u32[]{:S(2)}) copy-start(bf16[1,256,4,512]{3,2,1,0:T(4,128)(2,1)} %param.21) | copy-start | bytes 3145732
  219.9 6.9 %copy-start.20 = (bf16[1,256,4,256]{3,1,2,0:T(8,128)(2,1)S(1)}, bf16[1,256,4,256]{3,1,2,0:T(8,128)(2,1)}, u32[]{:S(2)}) copy-start(bf16[1,256,4,256]{3,1,2,0:T(8,128)(2,1)} %copy.168) | copy-start | bytes 1572868
  235.9 4.7 %copy-start.14 = (bf16[1024,512,1]{1,0,2:T(8,128)(2,1)S(1)}, bf16[1024,512,1]{1,0,2:T(8,128)(2,1)}, u32[]{:S(2)}) copy-start(bf16[1024,512,1]{1,0,2:T(8,128)(2,1)} %reshape.295) | copy-start | bytes 3145732
  240.6 3.8 copy-start.16
  246.8 179.7 %all-reduce.2.cloned.1.call-start = ((), (), s32[]{:S(2)}) async-start(), calls=%async_computation.6 | async-start | bytes 262144 | tf_op jit(solution)/shard_map/psum | solution.py:198
  346.7 82.7 %copy-start.1 = (bf16[512,1536]{1,0:T(8,128)(2,1)S(1)}, bf16[512,1536]{1,0:T(8,128)(2,1)}, u32[]{:S(2)}) copy-start(bf16[512,1536]{1,0:T(8,128)(2,1)} %param.17) | copy-start | bytes 4718596
Sparse Core Ops, SparseCore 0:
  247.0 99.7 reduce-scatter.1
  349.3 77.1 all-reduce.1
